TPU v7x, 32 devices: a whole 2x2x4 slice. The times are simulated.
32 devices in a mesh: pix: 16 (over z, y, x), mode: 2 (over core).
Axes of the slice: x: 2, y: 2, z: 4, core: 2. Of those that a mesh axis runs over, the one named last changes fastest.
Arguments:
- frames: float32 [384, 49152], P('mode', 'pix'), may hold values from -40 to 40
- basis: float32 [2048, 49152], P('mode', 'pix'), may hold values from -0.078125 to 0.078125
- annulus: int32 [64], P('pix'), may hold values from 0 to 7, as said below
- truncation: int32 [8], replicated, may hold values from 256 to 2048
Outputs:
- residual: float32 [384, 49152], P('mode', 'pix')
Inputs may be any that keep to these rules, and one draw needn't show every extreme that they name: Every annulus holds one block or more; the blocks of an annulus may lie anywhere in the image.
All inputs are finite; a program needn't handle non-finite values.
Results may differ from a plain program's by a relative error of at most 0.0001.
Values sent between devices are 32-bit elements; how exact they have to be, the bound alone decides.
No kernel may reach another device: no remote copies, remote signals or barrier semaphores. Data moves between devices by JAX's collectives and lax.ppermute only.
A program may use at most 128 MiB of HBM per device.

v0:
```python
import jax
import jax.numpy as jnp
from jax import lax
from jax.sharding import PartitionSpec as P

NA = 8


HIGHEST_PRECISION = lax.Precision.HIGHEST


def block_products(source, shaped, onehot):
    per_block = jnp.einsum("fbp,kbp->bfk", source, shaped, precision=HIGHEST_PRECISION)
    return jnp.einsum("ba,bfk->afk", onehot, per_block, precision=HIGHEST_PRECISION)


def local(frames, basis, annulus, truncation):
    gathered = lax.all_gather(frames, "mode", axis=0, tiled=True)
    total_frames, pix_dev = gathered.shape
    own_rows = frames.shape[0]
    blocks = annulus.shape[0]
    block_len = pix_dev // blocks
    modes_dev = basis.shape[0]
    onehot = (annulus[:, None] == jnp.arange(NA, dtype=jnp.int32)[None, :]).astype(jnp.float32)
    framed = gathered.reshape(total_frames, blocks, block_len)
    shaped = basis.reshape(modes_dev, blocks, block_len)
    local_sums = jnp.einsum(
        "ba,fb->af", onehot, jnp.sum(framed, axis=2), precision=HIGHEST_PRECISION
    )
    local_counts = jnp.sum(onehot, axis=0) * block_len
    mode_ids = lax.axis_index("mode") * modes_dev + jnp.arange(modes_dev, dtype=jnp.int32)
    retained = (mode_ids[None, :] < truncation[:, None]).astype(jnp.float32)
    annulus_totals, pixel_counts = lax.psum((local_sums, local_counts), "pix")
    annulus_means = annulus_totals / pixel_counts[:, None]
    centered = (
        framed
        - jnp.einsum("ba,af->fb", onehot, annulus_means, precision=HIGHEST_PRECISION)[:, :, None]
    )
    partial_value = block_products(centered, shaped, onehot)
    coefficients = lax.psum(partial_value, "pix")
    truncated = coefficients * retained[:, None, :]
    picked = jnp.einsum("ba,afk->bfk", onehot, truncated, precision=HIGHEST_PRECISION)
    term = jnp.einsum("bfk,kbp->fbp", picked, shaped, precision=HIGHEST_PRECISION)
    model_rows = lax.psum_scatter(
        term.reshape(own_rows * lax.axis_size("mode"), pix_dev),
        "mode",
        scatter_dimension=0,
        tiled=True,
    )
    own_means = lax.dynamic_slice_in_dim(
        annulus_means, lax.axis_index("mode") * own_rows, own_rows, 1
    )
    own_frames = frames.reshape(own_rows, blocks, block_len)
    own_centered = (
        own_frames
        - jnp.einsum("ba,af->fb", onehot, own_means, precision=HIGHEST_PRECISION)[:, :, None]
    )
    return (own_centered - model_rows.reshape(own_rows, blocks, block_len)).reshape(
        own_rows, pix_dev
    )


def solution(mesh):
    return jax.shard_map(
        local,
        mesh=mesh,
        in_specs=(P("mode", "pix"), P("mode", "pix"), P("pix"), P()),
        out_specs=P("mode", "pix"),
        check_vma=False,
    )
```

profile of v0, /device:TPU:13, one launch (start us, length us, event | category | flops | bytes accessed | tf_op | source)
XLA Modules:
  0.0 577.4 jit_solution(9454181733235314952)
XLA Ops:
  6.5 0.7 all-gather.2.cloned.1.call-update
  7.3 0.7 convert_reduce_fusion
  8.1 17.2 %all-gather.2.cloned.1.call-done = f32[384,3072]{1,0:T(8,128)} async-done(((f32[192,3072]{1,0:T(8,128)}), f32[384,3072]{1,0:T(8,128)}) %all-gather.2.cloned.1.call-update) | async-done | bytes 4718608 | tf_op jit(solution)/shard_map/all_gather | solution.py:18
  25.2 6.6 %reshape.45 = f32[384,4,768]{2,1,0:T(4,128)} reshape(f32[384,3072]{1,0:T(8,128)} %all-gather.2.cloned.1.call-done) | data formatting | bytes 9437184 | tf_op jit(solution)/shard_map/reshape | solution.py:25
  31.8 3.0 reduce_sum.18
  34.9 0.3 fusion.27
  35.2 53.3 %all-reduce = (f32[8,384]{1,0:T(8,128)S(1)}, f32[8]{0:T(128)S(1)}) all-reduce(f32[8,384]{1,0:T(8,128)S(1)} %fusion.27, f32[8]{0:T(128)S(1)} %broadcast_multiply_fusion), channel_id=1, replica_groups=mesh['pix'=16,'mode'=2] {'pix'}, use_global_device_ids=true, to_apply=%region_1.0 | all-reduce | flops 3080 | bytes 24640 | tf_op jit(solution)/shard_map/psum | solution.py:33
  88.5 0.2 fusion.23
  88.7 18.6 %fusion.2 = f32[4,384,1024]{2,1,0:T(8,128)S(1)} fusion(f32[128,4,8,768]{3,2,1,0:T(8,128)} %bitcast.26, f32[48,4,8,768]{3,2,1,0:T(8,128)} %bitcast.28, f32[384,4]{0,1:T(4,128)S(1)} %fusion.23), kind=kOutput, calls=%fused_computation.2 | convolution fusion | flops 14496694272 | bytes 23599104 | tf_op jit(solution)/shard_map/fbp,kbp->bfk/dot_general | solution.py:13
  107.3 11.6 %fusion.9 = f32[8,384,1024]{2,0,1:T(8,128)} fusion(f32[4,384,1024]{2,1,0:T(8,128)S(1)} %fusion.2, s32[4]{0:T(128)S(1)} %copy-done), kind=kOutput, calls=%fused_computation.9 | convolution fusion | flops 150994976 | bytes 18874384 | tf_op jit(solution)/shard_map/ba,bfk->afk/dot_general | solution.py:14
  119.0 0.2 reduce-scatter.4.cloned.1.call-start
  119.2 0.4 copy-done.1
  119.6 0.1 compare_convert_fusion
  119.7 373.4 %all-reduce.3.cloned.1.call-done = f32[8,384,1024]{2,0,1:T(8,128)} async-done(((f32[8,384,1024]{2,0,1:T(8,128)}), f32[8,384,1024]{2,0,1:T(8,128)}) %all-reduce.3.cloned.1.call-update) | async-done | bytes 12582928 | tf_op jit(solution)/shard_map/psum | solution.py:40
  493.0 9.3 %fusion.4 = f32[4,384,1024]{2,0,1:T(4,128)S(1)} fusion(f32[8,384,1024]{2,0,1:T(8,128)} %all-reduce.3.cloned.1.call-done, f32[8,1024]{1,0:T(8,128)S(1)} %compare_convert_fusion, s32[4]{0:T(128)S(1)} %copy-done), kind=kOutput, calls=%fused_computation.4 | convolution fusion | flops 154140704 | bytes 18907152 | tf_op jit(solution)/shard_map/ba,afk->bfk/dot_general | solution.py:42
  502.3 31.1 %fusion.15 = f32[384,4,768]{2,0,1:T(8,128)} fusion(f32[128,4,8,768]{3,2,1,0:T(8,128)} %bitcast.27, f32[4,384,1024]{2,0,1:T(4,128)S(1)} %fusion.4), kind=kOutput, calls=%fused_computation.17 | convolution fusion | flops 14495514624 | bytes 23592960 | tf_op jit(solution)/shard_map/bfk,kbp->fbp/dot_general | solution.py:43
  533.4 6.1 %copy.17 = f32[384,4,768]{0,2,1:T(8,128)} copy(f32[384,4,768]{2,0,1:T(8,128)} %fusion.15) | data formatting | bytes 9437184 | tf_op jit(solution)/shard_map/bfk,kbp->fbp/transpose | solution.py:43
  539.4 6.1 %copy.19 = f32[384,3072]{1,0:T(8,128)} copy(f32[384,3072]{0,1:T(8,128)} %bitcast.29) | data formatting | bytes 9437184
  545.6 2.2 copy.11
  547.8 0.2 fusion.20
  548.0 12.2 %reduce-scatter.4.cloned.1.call-done = f32[192,3072]{1,0:T(8,128)} async-done(((f32[384,3072]{1,0:T(8,128)}), f32[192,3072]{1,0:T(8,128)}) %reduce-scatter.4.cloned.1.call-update) | async-done | bytes 2359312
  560.2 3.4 copy.20
  563.6 4.0 fusion.13
  567.6 3.3 copy.18
  (10 shorter events, 0.2 us)
Async XLA Ops:
  6.5 18.7 %all-gather.2.cloned.1.call-start = ((), (), s32[]{:S(2)}) async-start(), calls=%async_computation.1 | async-start | bytes 7077888 | tf_op jit(solution)/shard_map/all_gather | solution.py:18
  7.3 485.7 %all-reduce.3.cloned.1.call-start = ((), (), s32[]{:S(2)}) async-start(), calls=%async_computation.2 | async-start | bytes 25165824 | tf_op jit(solution)/shard_map/psum | solution.py:40
  8.1 26.8 %copy-start = (s32[4]{0:T(128)S(1)}, s32[4]{0:T(128)}, u32[]{:S(2)}) copy-start(s32[4]{0:T(128)} %param.6) | copy-start | bytes 52
  118.9 0.7 copy-start.1
  119.0 441.2 %reduce-scatter.4.cloned.1.call-start = ((), (), s32[]{:S(2)}) async-start(), calls=%async_computation.3 | async-start | bytes 7077888
Sparse Core Ops, SparseCore 0:
  8.9 16.2 all-gather.1
  119.1 373.8 all-reduce.2
  545.7 14.4 reduce-scatter.3
where the time goes:
time: 579 us; the launch traced here: 577 us
  waiting for transfers between devices  403 us (70%)
  matrix products  71.3 us (12%)
  blocking collectives  53.3 us (9%)
  local copies, waits for them, and re-layouts  28.2 us (5%)
  between operations  13.2 us (2%)
  other arithmetic  7.9 us (1%)
    psum x1, waiting for transfers between devices, local(): coefficients = lax.psum(partial_value, 'pix')  373 us
    psum x1, blocking collectives, local(): annulus_totals, pixel_counts = lax.psum((local_sums, local_counts), 'pix')  53.3 us
    dot_general x1, matrix products, local(): jnp.einsum('bfk,kbp->fbp', picked, shaped, precision=HIGHEST_PRECISION)  31.1 us
    dot_general x1, matrix products, block_products(): jnp.einsum('fbp,kbp->bfk', source, shaped, precision=HIGHEST_PRECISION)  18.6 us
    all_gather x1, waiting for transfers between devices, local(): gathered = lax.all_gather(frames, 'mode', axis=0, tiled=True)  17.2 us
    unnamed x4, waiting for transfers between devices  12.9 us
    unnamed x7, local copies, waits for them, and re-layouts  12.2 us
    dot_general x1, matrix products, block_products(): jnp.einsum('ba,bfk->afk', onehot, per_block, precision=HIGHEST_PRECISION)  11.6 us
  transfers between devices with their start and end apart: 3, of which 3 were waited for; matrix products, arithmetic and copies ran while one was open for 1% of the time, Pallas kernels for 0%

commit v1 on v0

--- a/solution.py
+++ b/solution.py
@@ -12,6 +12,16 @@
 def block_products(source, shaped, onehot):
     per_block = jnp.einsum("fbp,kbp->bfk", source, shaped, precision=HIGHEST_PRECISION)
     return jnp.einsum("ba,bfk->afk", onehot, per_block, precision=HIGHEST_PRECISION)
+
+
+def butterfly_sum(value, axis):
+    size = lax.axis_size(axis)
+    step = 1
+    while step < size:
+        pairs = [(i, i ^ step) for i in range(size)]
+        value = value + lax.ppermute(value, axis, pairs)
+        step *= 2
+    return value
 
 
 def local(frames, basis, annulus, truncation):
@@ -30,7 +40,8 @@
     local_counts = jnp.sum(onehot, axis=0) * block_len
     mode_ids = lax.axis_index("mode") * modes_dev + jnp.arange(modes_dev, dtype=jnp.int32)
     retained = (mode_ids[None, :] < truncation[:, None]).astype(jnp.float32)
-    annulus_totals, pixel_counts = lax.psum((local_sums, local_counts), "pix")
+    packed = butterfly_sum(jnp.concatenate([local_sums, local_counts[:, None]], axis=1), "pix")
+    annulus_totals, pixel_counts = packed[:, :-1], packed[:, -1]
     annulus_means = annulus_totals / pixel_counts[:, None]
     centered = (
         framed

time: 579 us -> 524 us (0.905)
  blocking collectives: 53.3 us -> 0 us
  waiting for transfers between devices: 403 us -> 397 us
    psum x1 -> x0, blocking collectives: 53.3 us -> none  [local(): annulus_totals, pixel_counts = lax.psum((local_sums, local_counts), 'pix')]
    psum x1, waiting for transfers between devices: 373 us -> 360 us  [local(): coefficients = lax.psum(partial_value, 'pix')]
    ppermute x0 -> x4, waiting for transfers between devices: none -> 7.41 us  [butterfly_sum(): value = value + lax.ppermute(value, axis, pairs)]
  transfers between devices with their start and end apart: 3 -> 7, of which waited for: 3 -> 7; matrix products, arithmetic and copies ran while one was open for 1% -> 1% of each run, Pallas kernels for 0% -> 0%
where the time goes in v1:
time: 524 us; the launch traced here: 522 us
  waiting for transfers between devices  397 us (76%)
  matrix products  71.3 us (14%)
  local copies, waits for them, and re-layouts  28.4 us (5%)
  between operations  13.2 us (3%)
  other arithmetic  7.93 us (2%)
    psum x1, waiting for transfers between devices, local(): coefficients = lax.psum(partial_value, 'pix')  360 us
    dot_general x1, matrix products, local(): jnp.einsum('bfk,kbp->fbp', picked, shaped, precision=HIGHEST_PRECISION)  31.2 us
    dot_general x1, matrix products, block_products(): jnp.einsum('fbp,kbp->bfk', source, shaped, precision=HIGHEST_PRECISION)  18.6 us
    all_gather x1, waiting for transfers between devices, local(): gathered = lax.all_gather(frames, 'mode', axis=0, tiled=True)  17.1 us
    unnamed x4, waiting for transfers between devices  12.9 us
    unnamed x7, local copies, waits for them, and re-layouts  12.2 us
    dot_general x1, matrix products, block_products(): jnp.einsum('ba,bfk->afk', onehot, per_block, precision=HIGHEST_PRECISION)  11.6 us
  transfers between devices with their start and end apart: 7, of which 7 were waited for; matrix products, arithmetic and copies ran while one was open for 1% of the time, Pallas kernels for 0%

profile of v1, /device:TPU:13, one launch (start us, length us, event | category | flops | bytes accessed | tf_op | source)
XLA Modules:
  0.0 522.2 jit_solution(13193912470484974209)
XLA Ops:
  6.5 0.7 all-gather.2.cloned.1.call-update
  7.3 0.7 convert_reduce_fusion
  8.1 17.1 %all-gather.2.cloned.1.call-done = f32[384,3072]{1,0:T(8,128)} async-done(((f32[192,3072]{1,0:T(8,128)}), f32[384,3072]{1,0:T(8,128)}) %all-gather.2.cloned.1.call-update) | async-done | bytes 4718608 | tf_op jit(solution)/shard_map/all_gather | solution.py:28
  25.2 6.6 %reshape.53 = f32[384,4,768]{2,1,0:T(4,128)} reshape(f32[384,3072]{1,0:T(8,128)} %all-gather.2.cloned.1.call-done) | data formatting | bytes 9437184 | tf_op jit(solution)/shard_map/reshape | solution.py:35
  31.8 3.0 reduce_sum.18
  35.2 1.3 collective-permute-start
  36.5 1.4 collective-permute-done
  38.1 2.3 collective-permute-done.1
  40.7 2.3 collective-permute-done.2
  43.0 2.1 collective-permute-start.3
  45.2 1.4 collective-permute-done.3
  46.9 18.6 %fusion.2 = f32[4,384,1024]{2,1,0:T(8,128)S(1)} fusion(f32[128,4,8,768]{3,2,1,0:T(8,128)} %bitcast.28, f32[48,4,8,768]{3,2,1,0:T(8,128)} %bitcast.30, f32[384,4]{0,1:T(4,128)S(1)} %fusion.23), kind=kOutput, calls=%fused_computation.2 | convolution fusion | flops 14496694272 | bytes 23599104 | tf_op jit(solution)/shard_map/fbp,kbp->bfk/dot_general | solution.py:13
  65.5 11.6 %fusion.9 = f32[8,384,1024]{2,0,1:T(8,128)} fusion(f32[4,384,1024]{2,1,0:T(8,128)S(1)} %fusion.2, s32[4]{0:T(128)S(1)} %copy-done), kind=kOutput, calls=%fused_computation.9 | convolution fusion | flops 150994976 | bytes 18874384 | tf_op jit(solution)/shard_map/ba,bfk->afk/dot_general | solution.py:14
  77.4 0.4 copy-done.1
  77.9 359.8 %all-reduce.2.cloned.1.call-done = f32[8,384,1024]{2,0,1:T(8,128)} async-done(((f32[8,384,1024]{2,0,1:T(8,128)}), f32[8,384,1024]{2,0,1:T(8,128)}) %all-reduce.2.cloned.1.call-update) | async-done | bytes 12582928 | tf_op jit(solution)/shard_map/psum | solution.py:51
  437.7 9.3 %fusion.4 = f32[4,384,1024]{2,0,1:T(4,128)S(1)} fusion(f32[8,384,1024]{2,0,1:T(8,128)} %all-reduce.2.cloned.1.call-done, f32[8,1024]{1,0:T(8,128)S(1)} %compare_convert_fusion, s32[4]{0:T(128)S(1)} %copy-done), kind=kOutput, calls=%fused_computation.4 | convolution fusion | flops 154140704 | bytes 18907152 | tf_op jit(solution)/shard_map/ba,afk->bfk/dot_general | solution.py:53
  447.0 31.2 %fusion.15 = f32[384,4,768]{2,0,1:T(8,128)} fusion(f32[128,4,8,768]{3,2,1,0:T(8,128)} %bitcast.29, f32[4,384,1024]{2,0,1:T(4,128)S(1)} %fusion.4), kind=kOutput, calls=%fused_computation.17 | convolution fusion | flops 14495514624 | bytes 23592960 | tf_op jit(solution)/shard_map/bfk,kbp->fbp/dot_general | solution.py:54
  478.2 6.1 %copy.20 = f32[384,4,768]{0,2,1:T(8,128)} copy(f32[384,4,768]{2,0,1:T(8,128)} %fusion.15) | data formatting | bytes 9437184 | tf_op jit(solution)/shard_map/bfk,kbp->fbp/transpose | solution.py:54
  484.2 6.1 %copy.22 = f32[384,3072]{1,0:T(8,128)} copy(f32[384,3072]{0,1:T(8,128)} %bitcast.31) | data formatting | bytes 9437184
  490.4 2.2 copy.14
  492.8 12.2 %reduce-scatter.4.cloned.1.call-done = f32[192,3072]{1,0:T(8,128)} async-done(((f32[384,3072]{1,0:T(8,128)}), f32[192,3072]{1,0:T(8,128)}) %reduce-scatter.4.cloned.1.call-update) | async-done | bytes 2359312
  505.0 3.4 copy.23
  508.4 4.0 fusion.13
  512.3 3.3 copy.21
  (24 shorter events, 1.9 us)
Async XLA Ops:
  6.5 18.7 %all-gather.2.cloned.1.call-start = ((), (), s32[]{:S(2)}) async-start(), calls=%async_computation.1 | async-start | bytes 7077888 | tf_op jit(solution)/shard_map/all_gather | solution.py:28
  7.3 430.5 %all-reduce.2.cloned.1.call-start = ((), (), s32[]{:S(2)}) async-start(), calls=%async_computation.2 | async-start | bytes 25165824 | tf_op jit(solution)/shard_map/psum | solution.py:51
  8.1 26.7 %copy-start = (s32[4]{0:T(128)S(1)}, s32[4]{0:T(128)}, u32[]{:S(2)}) copy-start(s32[4]{0:T(128)} %param.6) | copy-start | bytes 52
  35.2 2.7 collective-permute-start
  37.9 2.6 collective-permute-start.1
  40.5 2.6 collective-permute-start.2
  43.0 3.5 collective-permute-start.3
  77.1 0.7 copy-start.1
  77.2 427.8 %reduce-scatter.4.cloned.1.call-start = ((), (), s32[]{:S(2)}) async-start(), calls=%async_computation.3 | async-start | bytes 7077888
Sparse Core Ops, SparseCore 0:
  8.9 16.2 all-gather.1
  77.3 360.3 all-reduce.1
  490.5 14.4 reduce-scatter.3

commit v2 on v1

--- a/solution.py
+++ b/solution.py
@@ -47,10 +47,18 @@
         framed
         - jnp.einsum("ba,af->fb", onehot, annulus_means, precision=HIGHEST_PRECISION)[:, :, None]
     )
-    partial_value = block_products(centered, shaped, onehot)
-    coefficients = lax.psum(partial_value, "pix")
-    truncated = coefficients * retained[:, None, :]
-    picked = jnp.einsum("ba,afk->bfk", onehot, truncated, precision=HIGHEST_PRECISION)
+    per_block = jnp.einsum("fbp,kbp->bfk", centered, shaped, precision=HIGHEST_PRECISION)
+    gathered_blocks = lax.all_to_all(per_block, "pix", 1, 0, tiled=True)
+    every_annulus = lax.all_gather(annulus, "pix", axis=0, tiled=True)
+    every_onehot = (every_annulus[:, None] == jnp.arange(NA, dtype=jnp.int32)[None, :]).astype(
+        jnp.float32
+    )
+    slice_coefficients = jnp.einsum(
+        "ba,bfk->afk", every_onehot, gathered_blocks, precision=HIGHEST_PRECISION
+    )
+    slice_truncated = slice_coefficients * retained[:, None, :]
+    outgoing = jnp.take(slice_truncated, every_annulus, axis=0)
+    picked = lax.all_to_all(outgoing, "pix", 0, 1, tiled=True)
     term = jnp.einsum("bfk,kbp->fbp", picked, shaped, precision=HIGHEST_PRECISION)
     model_rows = lax.psum_scatter(
         term.reshape(own_rows * lax.axis_size("mode"), pix_dev),

time: 524 us -> 453 us (0.86)
  waiting for transfers between devices: 397 us -> 42.4 us
  blocking collectives: 0 us -> 272 us
  local copies, waits for them, and re-layouts: 28.4 us -> 58.8 us
  matrix products: 71.3 us -> 41.2 us
  starting transfers between devices: 4.17 us -> 10.6 us
    psum x1 -> x0, waiting for transfers between devices: 360 us -> none  [local(): coefficients = lax.psum(partial_value, 'pix')]
    all_to_all x0 -> x1, blocking collectives: none -> 141 us  [local(): picked = lax.all_to_all(outgoing, 'pix', 0, 1, tiled=True)]
    unnamed x0 -> x1, blocking collectives: none -> 131 us
    all_to_all x0 -> x3, local copies, waits for them, and re-layouts: none -> 19 us  [the longest x2 15.3 us: local(): gathered_blocks = lax.all_to_all(per_block, 'pix', 1, 0, tiled=True)]
    dot_general x3 -> x2, matrix products: 39.5 us -> 23.1 us  [the longest x1 18.6 us: local(): jnp.einsum('fbp,kbp->bfk', centered, shaped, precision=HIGHEST_PRECISION)]
    dot_general x1, matrix products: 31.2 us -> 17.4 us  [local(): jnp.einsum('bfk,kbp->fbp', picked, shaped, precision=HIGHEST_PRECISION)]
    all_to_all x0 -> x1, starting transfers between devices: none -> 6.69 us  [local(): gathered_blocks = lax.all_to_all(per_block, 'pix', 1, 0, tiled=True)]
    dot_general x0 -> x1, local copies, waits for them, and re-layouts: none -> 6.68 us  [local(): jnp.einsum('fbp,kbp->bfk', centered, shaped, precision=HIGHEST_PRECISION)]
where the time goes in v2:
time: 453 us; the launch traced here: 451 us
  blocking collectives  272 us (60%)
  local copies, waits for them, and re-layouts  58.8 us (13%)
  waiting for transfers between devices  42.4 us (9%)
  matrix products  41.2 us (9%)
  between operations  14.2 us (3%)
  other arithmetic  11.6 us (3%)
  starting transfers between devices  10.6 us (2%)
    all_to_all x1, blocking collectives, local(): picked = lax.all_to_all(outgoing, 'pix', 0, 1, tiled=True)  141 us
    unnamed x1, blocking collectives  131 us
    dot_general x1, matrix products, local(): jnp.einsum('fbp,kbp->bfk', centered, shaped, precision=HIGHEST_PRECISION)  18.6 us
    dot_general x1, matrix products, local(): jnp.einsum('bfk,kbp->fbp', picked, shaped, precision=HIGHEST_PRECISION)  17.4 us
    all_gather x1, waiting for transfers between devices, local(): gathered = lax.all_gather(frames, 'mode', axis=0, tiled=True)  17.1 us
    all_to_all x2, local copies, waits for them, and re-layouts, local(): gathered_blocks = lax.all_to_all(per_block, 'pix', 1, 0, tiled=True)  15.3 us
    unnamed x18, local copies, waits for them, and re-layouts  12.9 us
    unnamed x3, waiting for transfers between devices  12.4 us
  transfers between devices with their start and end apart: 7, of which 7 were waited for; matrix products, arithmetic and copies ran while one was open for 1% of the time, Pallas kernels for 0%

profile of v2, /device:TPU:13, one launch (start us, length us, event | category | flops | bytes accessed | tf_op | source)
XLA Modules:
  0.0 451.0 jit_solution(14297415190474989145)
XLA Ops:
  8.1 17.1 %all-gather.2.cloned.1.call-done = f32[384,3072]{1,0:T(8,128)} async-done(((f32[192,3072]{1,0:T(8,128)}), f32[384,3072]{1,0:T(8,128)}) %all-gather.2.cloned.1.call-update) | async-done | bytes 4718608 | tf_op jit(solution)/shard_map/all_gather | solution.py:28
  25.2 6.6 %reshape.59 = f32[384,4,768]{2,1,0:T(4,128)} reshape(f32[384,3072]{1,0:T(8,128)} %all-gather.2.cloned.1.call-done) | data formatting | bytes 9437184 | tf_op jit(solution)/shard_map/reshape | solution.py:35
  31.8 3.0 reduce_sum.18
  38.1 2.3 collective-permute-done.1
  40.7 2.3 collective-permute-done.2
  46.9 18.6 %fusion.2 = f32[4,384,1024]{2,1,0:T(8,128)S(1)} fusion(f32[128,4,8,768]{3,2,1,0:T(8,128)} %bitcast.40, f32[48,4,8,768]{3,2,1,0:T(8,128)} %bitcast.45, f32[384,4]{0,1:T(4,128)S(1)} %fusion.17), kind=kOutput, calls=%fused_computation.3 | convolution fusion | flops 14496694272 | bytes 23599104 | tf_op jit(solution)/shard_map/fbp,kbp->bfk/dot_general | solution.py:50
  65.5 6.7 %copy.37 = f32[4,384,1024]{2,0,1:T(4,128)} copy(f32[4,384,1024]{2,1,0:T(8,128)S(1)} %fusion.2) | data formatting | bytes 12582912 | tf_op jit(solution)/shard_map/fbp,kbp->bfk/dot_general | solution.py:50
  72.2 6.7 %all-to-all-start = ((f32[4,384,1024]{2,0,1:T(4,128)}), f32[4,384,1024]{2,0,1:T(4,128)}, u32[]{:S(2)}, u32[]{:S(2)}) async-start(f32[4,384,1024]{2,0,1:T(4,128)} %copy.37), calls=%async_computation | async-start | bytes 12582912 | tf_op jit(solution)/shard_map/all_to_all | solution.py:51
  80.4 130.9 %all-reduce = s32[64]{0:T(128)S(1)} all-reduce(s32[64]{0:T(128)S(1)} %dynamic-update-slice), channel_id=1, replica_groups=mesh['pix'=16,'mode'=2] {'pix'}, use_global_device_ids=true, to_apply=%add | all-reduce | flops 64 | bytes 512
  211.5 5.5 %all-to-all-done = f32[4,384,1024]{2,0,1:T(4,128)} async-done(((f32[4,384,1024]{2,0,1:T(4,128)}), f32[4,384,1024]{2,0,1:T(4,128)}, u32[]{:S(2)}, u32[]{:S(2)}) %all-to-all-start) | async-done | bytes 6291488 | tf_op jit(solution)/shard_map/all_to_all | solution.py:51
  217.0 7.6 %copy.63 = f32[4,16,24,1024]{3,0,1,2:T(4,128)} copy(f32[4,16,24,1024]{3,0,2,1:T(4,128)} %bitcast.4) | data formatting | bytes 12582912 | tf_op jit(solution)/shard_map/all_to_all | solution.py:51
  224.6 7.7 %all_to_all.29 = f32[64,24,1024]{2,0,1:T(8,128)} reshape(f32[16,4,24,1024]{3,1,0,2:T(4,128)} %bitcast.46) | data formatting | bytes 12582912 | tf_op jit(solution)/shard_map/all_to_all | solution.py:51
  232.3 4.6 %convolution_multiply_fusion = f32[8,24,1024]{2,0,1:T(8,128)S(1)} fusion(f32[64,24,1024]{2,0,1:T(8,128)} %all_to_all.29, f32[8,1024]{1,0:T(8,128)S(1)} %compare_convert_fusion, s32[64]{0:T(128)S(1)} %all-reduce), kind=kOutput, calls=%fused_computation.15 | convolution fusion | flops 151192064 | bytes 7110912 | tf_op jit(solution)/shard_map/ba,bfk->afk/dot_general | solution.py:56
  237.3 3.6 gather_fusion
  240.9 3.7 broadcast_select_fusion
  244.6 141.1 %all_to_all.36 = f32[64,24,1024]{2,1,0:T(8,128)} all-to-all(f32[64,24,1024]{2,1,0:T(8,128)S(1)} %broadcast_select_fusion), channel_id=1, replica_groups=mesh['pix'=16,'mode'=2] {'pix'}, dimensions={0} | all-to-all | bytes 12582912 | tf_op jit(solution)/shard_map/all_to_all | solution.py:61
  385.7 3.7 copy.40
  389.7 17.4 %fusion.9 = f32[384,4,768]{2,0,1:T(8,128)} fusion(f32[4,384,1024]{2,1,0:T(8,128)S(1)} %bitcast.44, f32[128,4,8,768]{3,2,1,0:T(8,128)S(1)} %bitcast.43), kind=kOutput, calls=%fused_computation.14 | convolution fusion | flops 14495514624 | bytes 23592960 | tf_op jit(solution)/shard_map/bfk,kbp->fbp/dot_general | solution.py:62
  407.1 6.1 %copy.42 = f32[384,4,768]{0,2,1:T(8,128)} copy(f32[384,4,768]{2,0,1:T(8,128)} %fusion.9) | data formatting | bytes 9437184 | tf_op jit(solution)/shard_map/bfk,kbp->fbp/transpose | solution.py:62
  413.2 6.1 %copy.44 = f32[384,3072]{1,0:T(8,128)} copy(f32[384,3072]{0,1:T(8,128)} %bitcast.48) | data formatting | bytes 9437184
  421.8 11.7 %reduce-scatter.4.cloned.1.call-done = f32[192,3072]{1,0:T(8,128)} async-done(((f32[384,3072]{1,0:T(8,128)}), f32[192,3072]{1,0:T(8,128)}) %reduce-scatter.4.cloned.1.call-update) | async-done | bytes 2359312
  433.4 3.4 copy.45
  436.8 3.9 fusion.7
  440.8 3.3 copy.43
  (46 shorter events, 13.1 us)
Async XLA Ops:
  6.5 18.7 %all-gather.2.cloned.1.call-start = ((), (), s32[]{:S(2)}) async-start(), calls=%async_computation.3 | async-start | bytes 7077888 | tf_op jit(solution)/shard_map/all_gather | solution.py:28
  8.1 26.8 %copy-start.1 = (s32[4]{0:T(128)S(1)}, s32[4]{0:T(128)}, u32[]{:S(2)}) copy-start(s32[4]{0:T(128)} %param.6) | copy-start | bytes 52
  35.2 2.7 collective-permute-start
  37.9 2.6 collective-permute-start.1
  40.4 2.6 collective-permute-start.2
  43.0 3.5 collective-permute-start.3
  72.2 6.7 %copy-start.2 = (u32[32]{0:T(128)S(1)}, u32[32]{0:T(128)}, u32[]{:S(2)}) copy-start(u32[32]{0:T(128)} %constant.34) | copy-start | bytes 388
  72.2 139.2 %copy-start = (s32[8]{0:T(128)S(1)}, s32[8]{0:T(128)}, u32[]{:S(2)}) copy-start(s32[8]{0:T(128)} %param.7) | copy-start | bytes 100
  72.2 144.8 %all-to-all-start = ((f32[4,384,1024]{2,0,1:T(4,128)}), f32[4,384,1024]{2,0,1:T(4,128)}, u32[]{:S(2)}, u32[]{:S(2)}) async-start(f32[4,384,1024]{2,0,1:T(4,128)} %copy.37), calls=%async_computation | async-start | bytes 12582912 | tf_op jit(solution)/shard_map/all_to_all | solution.py:51
  78.9 354.6 %reduce-scatter.4.cloned.1.call-start = ((), (), s32[]{:S(2)}) async-start(), calls=%async_computation.4 | async-start | bytes 7077888
  244.6 144.8 %slice-start = ((s8[12582912]{0:T(1024)(128)(4,1)}), s8[4194304]{0:T(1024)(128)(4,1)S(1)}, s32[]{:S(2)}) async-start(s8[12582912]{0:T(1024)(128)(4,1)} %bitcast.41), calls=%async_computation.5 | async-start | bytes 8388608
  244.6 144.8 %slice-start.1 = ((s8[12582912]{0:T(1024)(128)(4,1)}), s8[4194304]{0:T(1024)(128)(4,1)S(1)}, s32[]{:S(2)}) async-start(s8[12582912]{0:T(1024)(128)(4,1)} %bitcast.41), calls=%async_computation.6 | async-start | bytes 8388608
  385.7 4.0 slice-start.2
Sparse Core Ops, SparseCore 0:
  8.9 16.2 all-gather.1
  419.5 13.9 reduce-scatter.3

commit v3 on v1

--- a/solution.py
+++ b/solution.py
@@ -4,14 +4,10 @@
 from jax.sharding import PartitionSpec as P
 
 NA = 8
+K_CHUNKS = 2
 
 
 HIGHEST_PRECISION = lax.Precision.HIGHEST
-
-
-def block_products(source, shaped, onehot):
-    per_block = jnp.einsum("fbp,kbp->bfk", source, shaped, precision=HIGHEST_PRECISION)
-    return jnp.einsum("ba,bfk->afk", onehot, per_block, precision=HIGHEST_PRECISION)
 
 
 def butterfly_sum(value, axis):
@@ -31,6 +27,7 @@
     blocks = annulus.shape[0]
     block_len = pix_dev // blocks
     modes_dev = basis.shape[0]
+    parts = lax.axis_size("pix")
     onehot = (annulus[:, None] == jnp.arange(NA, dtype=jnp.int32)[None, :]).astype(jnp.float32)
     framed = gathered.reshape(total_frames, blocks, block_len)
     shaped = basis.reshape(modes_dev, blocks, block_len)
@@ -38,20 +35,42 @@
         "ba,fb->af", onehot, jnp.sum(framed, axis=2), precision=HIGHEST_PRECISION
     )
     local_counts = jnp.sum(onehot, axis=0) * block_len
+    own_slot = (
+        lax.axis_index("pix") * blocks + jnp.arange(blocks, dtype=jnp.int32)
+    )[:, None] == jnp.arange(parts * blocks, dtype=jnp.int32)[None, :]
+    local_table = jnp.einsum(
+        "ba,bc->ac", onehot, own_slot.astype(jnp.float32), precision=HIGHEST_PRECISION
+    )
+    packed = butterfly_sum(
+        jnp.concatenate([local_sums, local_counts[:, None], local_table], axis=1), "pix"
+    )
+    annulus_totals = packed[:, :total_frames]
+    pixel_counts = packed[:, total_frames]
+    every_onehot = packed[:, total_frames + 1 :].T
+    every_annulus = jnp.einsum(
+        "ba,a->b", every_onehot, jnp.arange(NA, dtype=jnp.float32), precision=HIGHEST_PRECISION
+    ).astype(jnp.int32)
     mode_ids = lax.axis_index("mode") * modes_dev + jnp.arange(modes_dev, dtype=jnp.int32)
     retained = (mode_ids[None, :] < truncation[:, None]).astype(jnp.float32)
-    packed = butterfly_sum(jnp.concatenate([local_sums, local_counts[:, None]], axis=1), "pix")
-    annulus_totals, pixel_counts = packed[:, :-1], packed[:, -1]
     annulus_means = annulus_totals / pixel_counts[:, None]
     centered = (
         framed
         - jnp.einsum("ba,af->fb", onehot, annulus_means, precision=HIGHEST_PRECISION)[:, :, None]
     )
-    partial_value = block_products(centered, shaped, onehot)
-    coefficients = lax.psum(partial_value, "pix")
-    truncated = coefficients * retained[:, None, :]
-    picked = jnp.einsum("ba,afk->bfk", onehot, truncated, precision=HIGHEST_PRECISION)
-    term = jnp.einsum("bfk,kbp->fbp", picked, shaped, precision=HIGHEST_PRECISION)
+    chunk = modes_dev // K_CHUNKS
+    term = None
+    for c in range(K_CHUNKS):
+        piece = shaped[c * chunk : (c + 1) * chunk]
+        per_block = jnp.einsum("fbp,kbp->bfk", centered, piece, precision=HIGHEST_PRECISION)
+        gathered_blocks = lax.all_to_all(per_block, "pix", 1, 0, tiled=True)
+        slice_coefficients = jnp.einsum(
+            "ba,bfk->afk", every_onehot, gathered_blocks, precision=HIGHEST_PRECISION
+        )
+        slice_truncated = slice_coefficients * retained[:, None, c * chunk : (c + 1) * chunk]
+        outgoing = jnp.take(slice_truncated, every_annulus, axis=0)
+        picked = lax.all_to_all(outgoing, "pix", 0, 1, tiled=True)
+        part = jnp.einsum("bfk,kbp->fbp", picked, piece, precision=HIGHEST_PRECISION)
+        term = part if term is None else term + part
     model_rows = lax.psum_scatter(
         term.reshape(own_rows * lax.axis_size("mode"), pix_dev),
         "mode",

time: 524 us -> 456 us (0.87)
  waiting for transfers between devices: 397 us -> 200 us
  blocking collectives: 0 us -> 73.5 us
  local copies, waits for them, and re-layouts: 28.4 us -> 83.4 us
  matrix products: 71.3 us -> 51.3 us
  starting transfers between devices: 4.17 us -> 18.1 us
  other arithmetic: 7.93 us -> 14 us
    psum x1 -> x0, waiting for transfers between devices: 360 us -> none  [local(): coefficients = lax.psum(partial_value, 'pix')]
    all_to_all x0 -> x3, waiting for transfers between devices: none -> 166 us  [the longest x2 110 us: local(): gathered_blocks = lax.all_to_all(per_block, 'pix', 1, 0, tiled=True)]
    all_to_all x0 -> x1, blocking collectives: none -> 73.5 us  [local(): picked = lax.all_to_all(outgoing, 'pix', 0, 1, tiled=True)]
    dot_general x4 -> x8, matrix products: 70.6 us -> 50.6 us  [the longest x2 23.2 us: local(): jnp.einsum('bfk,kbp->fbp', picked, piece, precision=HIGHEST_PRECISION)]
    all_to_all x0 -> x6, local copies, waits for them, and re-layouts: none -> 16 us  [the longest x4 13.4 us: local(): gathered_blocks = lax.all_to_all(per_block, 'pix', 1, 0, tiled=True)]
    unnamed x7 -> x19, local copies, waits for them, and re-layouts: 12.2 us -> 26.8 us
    all_to_all x0 -> x3, starting transfers between devices: none -> 13.9 us  [the longest x2 9.15 us: local(): gathered_blocks = lax.all_to_all(per_block, 'pix', 1, 0, tiled=True)]
    slice x1 -> x3, local copies, waits for them, and re-layouts: 0.12 us -> 11.6 us  [the longest x1 10.8 us: local(): piece = shaped[c * chunk:(c + 1) * chunk]]
  transfers between devices with their start and end apart: 7 -> 9, of which waited for: 7 -> 8; matrix products, arithmetic and copies ran while one was open for 1% -> 14% of each run, Pallas kernels for 0% -> 0%
where the time goes in v3:
time: 456 us; the launch traced here: 454 us
  waiting for transfers between devices  200 us (44%)
  local copies, waits for them, and re-layouts  83.4 us (18%)
  blocking collectives  73.5 us (16%)
  matrix products  51.3 us (11%)
  starting transfers between devices  18.1 us (4%)
  other arithmetic  14 us (3%)
  between operations  13.6 us (3%)
    all_to_all x2, waiting for transfers between devices, local(): gathered_blocks = lax.all_to_all(per_block, 'pix', 1, 0, tiled=True)  110 us
    all_to_all x1, blocking collectives, local(): picked = lax.all_to_all(outgoing, 'pix', 0, 1, tiled=True)  73.5 us
    all_to_all x1, waiting for transfers between devices, local(): picked = lax.all_to_all(outgoing, 'pix', 0, 1, tiled=True)  56.4 us
    unnamed x19, local copies, waits for them, and re-layouts  26.8 us
    dot_general x2, matrix products, local(): jnp.einsum('bfk,kbp->fbp', picked, piece, precision=HIGHEST_PRECISION)  23.2 us
    dot_general x2, matrix products, local(): jnp.einsum('fbp,kbp->bfk', centered, piece, precision=HIGHEST_PRECISION)  21.9 us
    all_gather x1, waiting for transfers between devices, local(): gathered = lax.all_gather(frames, 'mode', axis=0, tiled=True)  16.2 us
    all_to_all x4, local copies, waits for them, and re-layouts, local(): gathered_blocks = lax.all_to_all(per_block, 'pix', 1, 0, tiled=True)  13.4 us
  transfers between devices with their start and end apart: 9, of which 8 were waited for; matrix products, arithmetic and copies ran while one was open for 14% of the time, Pallas kernels for 0%

profile of v3, /device:TPU:13, one launch (start us, length us, event | category | flops | bytes accessed | tf_op | source)
XLA Modules:
  0.0 453.6 jit_solution(18010114449177021959)
XLA Ops:
  9.0 16.2 %all-gather.2.cloned.1.call-done = f32[384,3072]{1,0:T(8,128)} async-done(((f32[192,3072]{1,0:T(8,128)}), f32[384,3072]{1,0:T(8,128)}) %all-gather.2.cloned.1.call-update) | async-done | bytes 4718608 | tf_op jit(solution)/shard_map/all_gather | solution.py:24
  25.2 6.6 %reshape.41 = f32[384,4,768]{2,1,0:T(4,128)} reshape(f32[384,3072]{1,0:T(8,128)} %all-gather.2.cloned.1.call-done) | data formatting | bytes 9437184 | tf_op jit(solution)/shard_map/reshape | solution.py:32
  45.2 10.8 %fusion.28 = (f32[512,3072]{1,0:T(8,128)}, f32[512,3072]{1,0:T(8,128)}) fusion(f32[1024,3072]{1,0:T(8,128)} %param.7), kind=kLoop, calls=%fused_computation.50 | loop fusion | bytes 25165824 | tf_op jit(solution)/shard_map/slice | solution.py:63
  56.1 6.6 %copy.74 = f32[512,3072]{0,1:T(8,128)} copy(f32[512,3072]{1,0:T(8,128)} %get-tuple-element.6) | data formatting | bytes 12582912
  63.0 11.0 %fusion = f32[4,384,512]{2,1,0:T(8,128)S(1)} fusion(f32[512,4,768]{0,2,1:T(8,128)} %bitcast.67, f32[48,4,8,768]{3,2,1,0:T(8,128)} %bitcast.69, f32[384,4]{0,1:T(4,128)S(1)} %fusion.14), kind=kOutput, calls=%fused_computation.4 | convolution fusion | flops 7248936960 | bytes 14161920 | tf_op jit(solution)/shard_map/fbp,kbp->bfk/dot_general | solution.py:64
  74.0 3.7 copy.60
  77.7 4.6 %all-to-all-start.2 = ((f32[4,384,512]{2,0,1:T(4,128)}), f32[4,384,512]{2,0,1:T(4,128)S(1)}, u32[]{:S(2)}, u32[]{:S(2)}) async-start(f32[4,384,512]{2,0,1:T(4,128)} %copy.60), calls=%async_computation.2 | async-start | bytes 6291456 | tf_op jit(solution)/shard_map/all_to_all | solution.py:65
  82.3 6.5 %copy.73 = f32[512,3072]{0,1:T(8,128)} copy(f32[512,3072]{1,0:T(8,128)} %get-tuple-element.7) | data formatting | bytes 12582912
  88.9 11.0 %fusion.1 = f32[4,384,512]{2,1,0:T(8,128)S(1)} fusion(f32[512,4,768]{0,2,1:T(8,128)} %bitcast.65, f32[48,4,8,768]{3,2,1,0:T(8,128)} %bitcast.70, f32[384,4]{0,1:T(4,128)S(1)} %fusion.14), kind=kOutput, calls=%fused_computation.5 | convolution fusion | flops 7248936960 | bytes 14161920 | tf_op jit(solution)/shard_map/fbp,kbp->bfk/dot_general | solution.py:64
  99.8 3.7 copy.53
  103.5 49.3 %all-to-all-done.2 = f32[4,384,512]{2,0,1:T(4,128)S(1)} async-done(((f32[4,384,512]{2,0,1:T(4,128)}), f32[4,384,512]{2,0,1:T(4,128)S(1)}, u32[]{:S(2)}, u32[]{:S(2)}) %all-to-all-start.2) | async-done | bytes 3145760 | tf_op jit(solution)/shard_map/all_to_all | solution.py:65
  152.8 4.6 %all-to-all-start = ((f32[4,384,512]{2,0,1:T(4,128)}), f32[4,384,512]{2,0,1:T(4,128)}, u32[]{:S(2)}, u32[]{:S(2)}) async-start(f32[4,384,512]{2,0,1:T(4,128)} %copy.53), calls=%async_computation | async-start | bytes 6291456 | tf_op jit(solution)/shard_map/all_to_all | solution.py:65
  167.0 60.4 %all-to-all-done = f32[4,384,512]{2,0,1:T(4,128)} async-done(((f32[4,384,512]{2,0,1:T(4,128)}), f32[4,384,512]{2,0,1:T(4,128)}, u32[]{:S(2)}, u32[]{:S(2)}) %all-to-all-start) | async-done | bytes 3145760 | tf_op jit(solution)/shard_map/all_to_all | solution.py:65
  227.4 4.4 copy.82
  242.8 5.3 %broadcast_select_fusion = (f32[64,24,512]{2,1,0:T(8,128)}, f32[64,24,512]{2,1,0:T(8,128)S(1)}) fusion(f32[64,24,512]{2,1,0:T(8,128)} %gather_fusion.1, pred[64]{0:T(512)(128)(4,1)S(1)} %copy-done.6, f32[64,24,512]{2,1,0:T(8,128)} %gather_fusion), kind=kLoop, calls=%fused_computation.12 | loop fusion | flops 1572864 | bytes 12582976 | tf_op jit(solution)/shard_map/jit(_take)/select_n | solution.py:70
  248.1 73.5 %all_to_all.72 = f32[64,24,512]{2,1,0:T(8,128)} all-to-all(f32[64,24,512]{2,1,0:T(8,128)S(1)} %get-tuple-element.11), channel_id=1, replica_groups=mesh['pix'=16,'mode'=2] {'pix'}, dimensions={0} | all-to-all | bytes 6291456 | tf_op jit(solution)/shard_map/all_to_all | solution.py:71
  321.6 4.8 %all-to-all-start.3 = ((f32[64,24,512]{2,1,0:T(8,128)}), f32[64,24,512]{2,1,0:T(8,128)S(1)}, u32[]{:S(2)}, u32[]{:S(2)}) async-start(f32[64,24,512]{2,1,0:T(8,128)} %get-tuple-element.10), calls=%async_computation.3 | async-start | bytes 6291456 | tf_op jit(solution)/shard_map/all_to_all | solution.py:71
  328.9 11.5 %fusion.30 = f32[4,384,768]{2,1,0:T(8,128)} fusion(f32[4,384,512]{2,1,0:T(8,128)S(1)} %bitcast.73, f32[512,4,768]{0,2,1:T(8,128)} %bitcast.66), kind=kOutput, calls=%fused_computation.52 | convolution fusion | flops 7247757312 | bytes 14155776 | tf_op jit(solution)/shard_map/bfk,kbp->fbp/dot_general | solution.py:72
  340.4 56.4 %all-to-all-done.3 = f32[64,24,512]{2,1,0:T(8,128)S(1)} async-done(((f32[64,24,512]{2,1,0:T(8,128)}), f32[64,24,512]{2,1,0:T(8,128)S(1)}, u32[]{:S(2)}, u32[]{:S(2)}) %all-to-all-start.3) | async-done | bytes 3145760 | tf_op jit(solution)/shard_map/all_to_all | solution.py:71
  399.1 11.7 %add_bitcast_fusion = f32[384,4,768]{2,0,1:T(8,128)} fusion(f32[4,384,768]{2,1,0:T(8,128)S(1)} %copy-done, f32[4,384,512]{2,1,0:T(8,128)S(1)} %bitcast.72, f32[512,4,768]{0,2,1:T(8,128)} %bitcast.68), kind=kOutput, calls=%fused_computation.3 | convolution fusion | flops 7248936960 | bytes 18874368 | tf_op jit(solution)/shard_map/bfk,kbp->fbp/dot_general | solution.py:72
  410.9 6.1 %copy.65 = f32[384,4,768]{0,2,1:T(8,128)} copy(f32[384,4,768]{2,0,1:T(8,128)} %add_bitcast_fusion) | data formatting | bytes 9437184 | tf_op jit(solution)/shard_map/add | solution.py:73
  416.9 6.0 %copy.71 = f32[384,3072]{1,0:T(8,128)} copy(f32[384,3072]{0,1:T(8,128)} %bitcast.71) | data formatting | bytes 9437184
  425.5 10.6 %reduce-scatter.4.cloned.1.call-done = f32[192,3072]{1,0:T(8,128)} async-done(((f32[384,3072]{1,0:T(8,128)}), f32[192,3072]{1,0:T(8,128)}) %reduce-scatter.4.cloned.1.call-update) | async-done | bytes 2359312
  439.5 3.9 fusion.2
  (61 shorter events, 50.8 us)
Async XLA Ops:
  6.5 18.7 %all-gather.2.cloned.1.call-start = ((), (), s32[]{:S(2)}) async-start(), calls=%async_computation.5 | async-start | bytes 7077888 | tf_op jit(solution)/shard_map/all_gather | solution.py:24
  31.8 3.1 copy-start.4
  35.2 2.6 collective-permute-start
  37.9 2.6 collective-permute-start.1
  40.5 2.6 collective-permute-start.2
  43.1 19.5 %collective-permute-start.3 = (f32[8,449]{1,0:T(8,128)S(1)}, f32[8,449]{1,0:T(8,128)S(1)}, u32[]{:S(2)}, u32[]{:S(2)}) collective-permute-start(f32[8,449]{1,0:T(8,128)S(1)} %add.53), channel_id=1, source_target_pairs={{0,16},{2,18},{4,20},{6,22},{8,24},{10,26},{12,28},{14,30},{16,0},... | collective-permute-start | bytes 43112 | tf_op jit(solution)/shard_map/ppermute | solution.py:18
  62.8 11.2 %copy-start.1 = (f32[8,384]{1,0:T(8,128)}, f32[8,384]{1,0:T(8,128)S(1)}, u32[]{:S(2)}) copy-start(f32[8,384]{1,0:T(8,128)S(1)} %slice_divide_fusion) | copy-start | bytes 36868
  77.7 75.0 %all-to-all-start.2 = ((f32[4,384,512]{2,0,1:T(4,128)}), f32[4,384,512]{2,0,1:T(4,128)S(1)}, u32[]{:S(2)}, u32[]{:S(2)}) async-start(f32[4,384,512]{2,0,1:T(4,128)} %copy.60), calls=%async_computation.2 | async-start | bytes 6291456 | tf_op jit(solution)/shard_map/all_to_all | solution.py:65
  103.5 53.9 %copy-start.3 = (s32[8]{0:T(128)S(1)}, s32[8]{0:T(128)}, u32[]{:S(2)}) copy-start(s32[8]{0:T(128)} %param.9) | copy-start | bytes 100
  152.8 74.6 %all-to-all-start = ((f32[4,384,512]{2,0,1:T(4,128)}), f32[4,384,512]{2,0,1:T(4,128)}, u32[]{:S(2)}, u32[]{:S(2)}) async-start(f32[4,384,512]{2,0,1:T(4,128)} %copy.53), calls=%async_computation | async-start | bytes 6291456 | tf_op jit(solution)/shard_map/all_to_all | solution.py:65
  240.1 2.7 copy-start.6
  321.6 75.2 %all-to-all-start.3 = ((f32[64,24,512]{2,1,0:T(8,128)}), f32[64,24,512]{2,1,0:T(8,128)S(1)}, u32[]{:S(2)}, u32[]{:S(2)}) async-start(f32[64,24,512]{2,1,0:T(8,128)} %get-tuple-element.10), calls=%async_computation.3 | async-start | bytes 6291456 | tf_op jit(solution)/shard_map/all_to_all | solution.py:71
  326.4 109.7 %reduce-scatter.4.cloned.1.call-start = ((), (), s32[]{:S(2)}) async-start(), calls=%async_computation.6 | async-start | bytes 7077888
  396.8 2.3 copy-start
  423.0 2.3 copy-start.2
  423.0 2.3 copy-start.5
Sparse Core Ops, SparseCore 0:
  8.9 16.2 all-gather.1
  423.1 12.9 reduce-scatter.3
